TPU v7x, 32 devices: a whole 2x2x4 slice. The times are simulated.
32 devices in a mesh: dp: 4 (over z), vocab: 8 (over y, x, core).
Axes of the slice: x: 2, y: 2, z: 4, core: 2. Of those that a mesh axis runs over, the one named last changes fastest.
Arguments:
- hidden: bfloat16 [512, 8192], P('dp', 'vocab'), may hold values from -8 to 8
- out_weight: bfloat16 [19456, 8192], P('vocab', 'dp'), may hold values from -0.397747564 to 0.397747564
- token_blocks: int32 [8, 4, 16], P('vocab'), may hold values from 0 to 18, as said below
- counts: int32 [8, 4], P('vocab'), may hold values from 4 to 16, as said below
Outputs:
- allowed_logprob: float32 [8, 4, 16, 128, 128], P('vocab', 'dp')
- expected: float32 [512, 8192], P('vocab', 'dp')
Inputs may be any that keep to these rules, and one draw needn't show every extreme that they name: token_blocks[j, b, s] names one of the 19 token blocks of shard j; the entries of one list are distinct; slots at or past counts[j, b] carry no meaning. `counts`: for every beam block, some shard allows exactly 16 slots.
All inputs are finite; a program needn't handle non-finite values.
Results may differ from a plain program's by a relative error of at most 0.0021.
Values may be sent and summed in bfloat16 or wider, within the bound.
No kernel may reach another device: no remote copies, remote signals or barrier semaphores. Data moves between devices by JAX's collectives and lax.ppermute only.
A program may use at most 128 MiB of HBM per device.

v0:
```python
import jax
import jax.numpy as jnp
from jax import lax
from jax.sharding import PartitionSpec as P

TB = 128
BB = 128
MOST = 16


def per_device(hidden, out_weight, token_blocks, counts):
    vocab_here, columns_here = out_weight.shape
    width = hidden.shape[1] * lax.psum(1, "vocab")
    n_tb = vocab_here // TB
    block_lists = token_blocks[0]
    block_counts = counts[0]
    n_blk = block_lists.shape[0]
    own_blocks = hidden.shape[0] // BB
    first_block = lax.axis_index("dp") * own_blocks
    own_counts = lax.dynamic_slice_in_dim(block_counts, first_block, own_blocks, 0)
    beam_rows = lax.all_gather(hidden, "vocab", axis=1, tiled=True)
    beam_columns = lax.all_to_all(beam_rows, "dp", split_axis=1, concat_axis=0, tiled=True)
    with jax.named_scope("dense_logits"):
        full = jnp.einsum("bd,vd->bv", beam_columns, out_weight, preferred_element_type=jnp.float32)
        full4 = full.reshape(n_blk, BB, n_tb, TB)
        rows = jnp.arange(n_blk, dtype=jnp.int32)[:, None]
        picked = full4[rows, :, block_lists, :]
    logits = lax.psum_scatter(picked, "dp", scatter_dimension=0, tiled=True)
    with jax.named_scope("softmax_stats"):
        live = jnp.arange(MOST, dtype=jnp.int32)[None, :] < own_counts[:, None]
        live_mask = live[:, :, None, None]
        masked = jnp.where(live_mask, logits, -jnp.inf)
        local_max = jnp.max(masked, axis=(1, 3))
        local_total = jnp.sum(jnp.exp(masked - local_max[:, None, :, None]), axis=(1, 3))
        stats = lax.all_gather(jnp.stack([local_max, local_total]), "vocab", axis=0)
        beam_max = jnp.max(stats[:, 0], axis=0)
        beam_total = jnp.sum(stats[:, 1] * jnp.exp(stats[:, 0] - beam_max[None]), axis=0)
        shifted = logits - beam_max[:, None, :, None] - jnp.log(beam_total)[:, None, :, None]
        allowed_logprob = jnp.where(live_mask, shifted, 0.0)
        probabilities = jnp.where(live_mask, jnp.exp(shifted), 0.0).astype(jnp.bfloat16)
    prob_part = lax.all_gather(probabilities, "dp", axis=0, tiled=True)
    with jax.named_scope("dense_expected"):
        onehot = (
            block_lists[:, :, None] == jnp.arange(n_tb, dtype=jnp.int32)[None, None, :]
        ).astype(jnp.bfloat16)
        spread = jnp.einsum(
            "bsk,bsrt->brkt", onehot, prob_part, preferred_element_type=jnp.float32
        ).astype(jnp.bfloat16)
        embedding_part = jnp.einsum(
            "bv,vd->bd",
            spread.reshape(n_blk * BB, n_tb * TB),
            out_weight,
            preferred_element_type=jnp.float32,
        )
    summed = lax.psum_scatter(embedding_part, "vocab", scatter_dimension=0, tiled=True)
    squares = lax.psum(jnp.sum(summed * summed, axis=1), "dp")
    expected = summed * lax.rsqrt(squares / width + 1e-06)[:, None]
    return (allowed_logprob[None], expected)


def solution(mesh):
    in_specs = (P("dp", "vocab"), P("vocab", "dp"), P("vocab", None, None), P("vocab", None))
    out_specs = (P("vocab", "dp", None, None, None), P("vocab", "dp"))
    return jax.shard_map(
        per_device, mesh=mesh, in_specs=in_specs, out_specs=out_specs, check_vma=False
    )
```

profile of v0, /device:TPU:0, one launch (start us, length us, event | category | flops | bytes accessed | tf_op | source)
XLA Modules:
  0.0 333.0 jit_solution(18080191292290261255)
XLA Ops:
  7.2 0.0 copy-start
  7.2 0.0 all-gather.4.cloned.1.call-start
  7.2 1.8 copy.15
  9.0 0.0 all-gather.4.cloned.1.call-update
  9.0 31.9 %all-gather.4.cloned.1.call-done = bf16[128,8192]{0,1:T(8,128)(2,1)} async-done(((bf16[128,1024]{0,1:T(8,128)(2,1)}), bf16[128,8192]{0,1:T(8,128)(2,1)}) %all-gather.4.cloned.1.call-update) | async-done | bytes 2097168 | tf_op jit(solution)/shard_map/all_gather | solution.py:21
  41.0 0.0 copy-start.1
  41.0 4.0 %copy.16 = bf16[128,4,2048]{2,0,1:T(8,128)(2,1)} copy(bf16[128,4,2048]{0,2,1:T(8,128)(2,1)} %bitcast.42) | data formatting | bytes 4194304 | tf_op jit(solution)/shard_map/all_to_all | solution.py:22
  45.0 4.6 %all-to-all-start = ((bf16[128,4,2048]{2,0,1:T(8,128)(2,1)}), bf16[128,4,2048]{2,0,1:T(8,128)(2,1)S(1)}, u32[]{:S(2)}, u32[]{:S(2)}) async-start(bf16[128,4,2048]{2,0,1:T(8,128)(2,1)} %copy.16), calls=%async_computation | async-start | bytes 4194304 | tf_op jit(solution)/shard_map/all_to_all | solution.py:22
  49.6 0.0 reduce-scatter.3.cloned.1.call-start
  49.6 0.0 copy-done.1
  49.6 0.1 reshape.130
  49.7 48.5 %all-to-all-done = bf16[128,4,2048]{2,0,1:T(8,128)(2,1)S(1)} async-done(((bf16[128,4,2048]{2,0,1:T(8,128)(2,1)}), bf16[128,4,2048]{2,0,1:T(8,128)(2,1)S(1)}, u32[]{:S(2)}, u32[]{:S(2)}) %all-to-all-start) | async-done | bytes 2097184 | tf_op jit(solution)/shard_map/all_to_all | solution.py:22
  98.2 9.9 %fusion.3 = f32[4,128,19,128]{3,1,2,0:T(8,128)} fusion(bf16[19,128,2048,1]{2,1,0,3:T(8,128)(2,1)} %bitcast.50, bf16[128,4,2048]{2,0,1:T(8,128)(2,1)S(1)} %all-to-all-done), kind=kOutput, calls=%fused_computation.5 | convolution fusion | flops 5100273664 | bytes 17039360 | tf_op jit(solution)/shard_map/dense_logits/bd,vd->bv/dot_general | solution.py:24
  108.1 5.3 %gather_fusion = f32[64,128,128]{2,1,0:T(8,128)} fusion(f32[4,128,19,128]{3,1,2,0:T(8,128)} %fusion.3, s32[64]{0:T(128)S(1)} %reshape.130), kind=kCustom, calls=%fused_computation | custom fusion | bytes 8389120 | tf_op jit(solution)/shard_map/dense_logits/gather | solution.py:27
  113.4 0.0 reduce-scatter.3.cloned.1.call-update
  113.4 0.0 all-gather.6.cloned.1.call-start
  113.4 0.0 copy-done
  113.4 0.6 constant_dynamic-slice_fusion
  114.0 0.6 iota_compare_fusion.1
  114.7 73.8 %reduce-scatter.3.cloned.1.call-done = f32[1,16,128,128]{3,2,1,0:T(8,128)} async-done(((f32[4,16,128,128]{3,2,1,0:T(8,128)}), f32[1,16,128,128]{3,2,1,0:T(8,128)}) %reduce-scatter.3.cloned.1.call-update) | async-done | bytes 1048592 | tf_op jit(solution)/shard_map/reduce_scatter | solution.py:28
  188.5 1.4 select_reduce_fusion
  189.9 1.6 exponential_reduce_fusion
  191.5 8.9 %all-gather = f32[16,1,128]{2,1,0:T(1,128)S(1)} all-gather(f32[2,1,128]{2,1,0:T(1,128)S(1)} %pad_maximum_fusion), channel_id=2, replica_groups=mesh['dp'=4,'vocab'=8] {'vocab'}, dimensions={0}, use_global_device_ids=true | all-gather | bytes 9216 | tf_op jit(solution)/shard_map/softmax_stats/all_gather | solution.py:35
  200.4 2.8 select_convert_fusion
  203.2 0.0 all-gather.6.cloned.1.call-update
  203.3 0.0 reduce-scatter.5.cloned.1.call-start
  203.3 45.4 %all-gather.6.cloned.1.call-done = bf16[4,16,128,128]{3,2,1,0:T(8,128)(2,1)} async-done(((bf16[1,16,128,128]{3,2,1,0:T(8,128)(2,1)}), bf16[4,16,128,128]{3,2,1,0:T(8,128)(2,1)}) %all-gather.6.cloned.1.call-update) | async-done | bytes 2097168 | tf_op jit(solution)/shard_map/all_gather | solution.py:41
  248.7 3.3 convolution_convert_fusion
  251.9 9.5 %fusion = f32[512,2048]{1,0:T(8,128)} fusion(bf16[2432,2048]{1,0:T(8,128)(2,1)} %param.5, bf16[64,8,19,128]{3,2,1,0:T(8,128)(2,1)S(1)} %bitcast.41), kind=kOutput, calls=%fused_computation.1 | convolution fusion | flops 5100273664 | bytes 16646144 | tf_op jit(solution)/shard_map/dense_expected/bv,vd->bd/dot_general | solution.py:49
  261.5 0.0 reduce-scatter.5.cloned.1.call-update
  261.5 50.1 %reduce-scatter.5.cloned.1.call-done = f32[64,2048]{1,0:T(8,128)} async-done(((f32[512,2048]{1,0:T(8,128)}), f32[64,2048]{1,0:T(8,128)}) %reduce-scatter.5.cloned.1.call-update) | async-done | bytes 524304 | tf_op jit(solution)/shard_map/reduce_scatter | solution.py:55
  311.6 1.2 multiply_reduce_fusion
  312.8 11.7 %psum.7 = f32[64]{0:T(128)S(1)} all-reduce(f32[64]{0:T(128)S(1)} %multiply_reduce_fusion), channel_id=1, replica_groups=mesh['dp'=4,'vocab'=8] {'dp'}, use_global_device_ids=true, to_apply=%region_7.8 | all-reduce | flops 64 | bytes 512 | tf_op jit(solution)/shard_map/psum | solution.py:56
  324.5 1.9 broadcast_multiply_fusion
  (7 shorter events, 0.1 us)
Async XLA Ops:
  7.2 106.3 %copy-start = (s32[1,4]{1,0:T(1,128)S(1)}, s32[1,4]{1,0:T(1,128)}, u32[]{:S(2)}) copy-start(s32[1,4]{1,0:T(1,128)} %param.7) | copy-start | bytes 52
  7.2 33.8 %all-gather.4.cloned.1.call-start = ((), (), s32[]{:S(2)}) async-start(), calls=%async_computation.3 | async-start | bytes 2359296 | tf_op jit(solution)/shard_map/all_gather | solution.py:21
  41.0 8.6 %copy-start.1 = (s32[1,4,16]{2,1,0:T(4,128)S(1)}, s32[1,4,16]{2,1,0:T(4,128)}, u32[]{:S(2)}) copy-start(s32[1,4,16]{2,1,0:T(4,128)} %param.6) | copy-start | bytes 772
  45.0 53.2 %all-to-all-start = ((bf16[128,4,2048]{2,0,1:T(8,128)(2,1)}), bf16[128,4,2048]{2,0,1:T(8,128)(2,1)S(1)}, u32[]{:S(2)}, u32[]{:S(2)}) async-start(bf16[128,4,2048]{2,0,1:T(8,128)(2,1)} %copy.16), calls=%async_computation | async-start | bytes 4194304 | tf_op jit(solution)/shard_map/all_to_all | solution.py:22
  49.6 138.9 %reduce-scatter.3.cloned.1.call-start = ((), (), s32[]{:S(2)}) async-start(), calls=%async_computation.4 | async-start | bytes 5242880 | tf_op jit(solution)/shard_map/reduce_scatter | solution.py:28
  113.4 135.3 %all-gather.6.cloned.1.call-start = ((), (), s32[]{:S(2)}) async-start(), calls=%async_computation.5 | async-start | bytes 2621440 | tf_op jit(solution)/shard_map/all_gather | solution.py:41
  203.3 108.3 %reduce-scatter.5.cloned.1.call-start = ((), (), s32[]{:S(2)}) async-start(), calls=%async_computation.6 | async-start | bytes 4718592 | tf_op jit(solution)/shard_map/reduce_scatter | solution.py:55
Sparse Core Ops, SparseCore 0:
  10.4 30.4 all-gather.3
  113.5 74.9 reduce-scatter.2
  203.4 45.2 all-gather.5
  261.6 49.9 reduce-scatter.4
where the time goes:
time: 334 us; the launch traced here: 333 us
  waiting for transfers between devices  250 us (75%)
  matrix products  22.7 us (7%)
  blocking collectives  20.6 us (6%)
  between operations  13.8 us (4%)
  local copies, waits for them, and re-layouts  11.8 us (4%)
  other arithmetic  9.65 us (3%)
  starting transfers between devices  4.72 us (1%)
    reduce_scatter x1, waiting for transfers between devices, per_device(): logits = lax.psum_scatter(picked, 'dp', scatter_dimension=0, tiled=True)  73.8 us
    reduce_scatter x1, waiting for transfers between devices, per_device(): lax.psum_scatter(embedding_part, 'vocab', scatter_dimension=0, tiled=True)  50.1 us
    all_to_all x1, waiting for transfers between devices, per_device(): lax.all_to_all(beam_rows, 'dp', split_axis=1, concat_axis=0, tiled=True)  48.5 us
    all_gather x1, waiting for transfers between devices, per_device(): prob_part = lax.all_gather(probabilities, 'dp', axis=0, tiled=True)  45.4 us
    all_gather x1, waiting for transfers between devices, per_device(): beam_rows = lax.all_gather(hidden, 'vocab', axis=1, tiled=True)  31.9 us
    psum x1, blocking collectives, per_device(): squares = lax.psum(jnp.sum(summed * summed, axis=1), 'dp')  11.7 us
    dot_general x1, matrix products, per_device(): jnp.einsum('bd,vd->bv', beam_columns, out_weight, preferred_element_type=...  9.91 us
    dot_general x1, matrix products, per_device(): jnp.einsum('bv,vd->bd', spread.reshape(n_blk * BB, n_tb * TB), out_weight...  9.53 us
  transfers between devices with their start and end apart: 5, of which 5 were waited for; matrix products, arithmetic and copies ran while one was open for 0% of the time, Pallas kernels for 0%

commit v1 on v0

--- a/solution.py
+++ b/solution.py
@@ -38,7 +38,23 @@
         shifted = logits - beam_max[:, None, :, None] - jnp.log(beam_total)[:, None, :, None]
         allowed_logprob = jnp.where(live_mask, shifted, 0.0)
         probabilities = jnp.where(live_mask, jnp.exp(shifted), 0.0).astype(jnp.bfloat16)
-    prob_part = lax.all_gather(probabilities, "dp", axis=0, tiled=True)
+    ways, here, step = (lax.axis_size("dp"), lax.axis_index("dp"), probabilities.shape[0])
+    lengths = [n * ways if d == 0 else n for d, n in enumerate(probabilities.shape)]
+    full_2 = lax.dynamic_update_slice_in_dim(
+        jnp.zeros(lengths, probabilities.dtype), probabilities, here * step, axis=0
+    )
+    going_up = going_down = probabilities
+    for far in range(1, ways // 2 + 1):
+        going_up = lax.ppermute(going_up, "dp", [(d, (d + 1) % ways) for d in range(ways)])
+        full_2 = lax.dynamic_update_slice_in_dim(
+            full_2, going_up, (here - far) % ways * step, axis=0
+        )
+        if 2 * far < ways:
+            going_down = lax.ppermute(going_down, "dp", [(d, (d - 1) % ways) for d in range(ways)])
+            full_2 = lax.dynamic_update_slice_in_dim(
+                full_2, going_down, (here + far) % ways * step, axis=0
+            )
+    prob_part = full_2
     with jax.named_scope("dense_expected"):
         onehot = (
             block_lists[:, :, None] == jnp.arange(n_tb, dtype=jnp.int32)[None, None, :]

time: 334 us -> 323 us (0.967)
  waiting for transfers between devices: 250 us -> 227 us
  starting transfers between devices: 4.72 us -> 18.6 us
    all_gather x1 -> x0, waiting for transfers between devices: 45.4 us -> none  [per_device(): prob_part = lax.all_gather(probabilities, 'dp', axis=0, tiled=True)]
    ppermute x0 -> x3, waiting for transfers between devices: none -> 23.2 us  [the longest x2 23.2 us: per_device(): lax.ppermute(going_up, 'dp', [(d, (d + 1) % ways) for d in range(ways)])]
    ppermute x0 -> x3, starting transfers between devices: none -> 13.8 us  [the longest x2 11.5 us: per_device(): lax.ppermute(going_up, 'dp', [(d, (d + 1) % ways) for d in range(ways)])]
  transfers between devices with their start and end apart: 5 -> 7, of which waited for: 5 -> 6; matrix products, arithmetic and copies ran while one was open for 0% -> 1% of each run, Pallas kernels for 0% -> 0%
where the time goes in v1:
time: 323 us; the launch traced here: 322 us
  waiting for transfers between devices  227 us (70%)
  blocking collectives  20.6 us (6%)
  matrix products  20.5 us (6%)
  starting transfers between devices  18.6 us (6%)
  between operations  13.8 us (4%)
  local copies, waits for them, and re-layouts  13.5 us (4%)
  other arithmetic  8.34 us (3%)
    reduce_scatter x1, waiting for transfers between devices, per_device(): logits = lax.psum_scatter(picked, 'dp', scatter_dimension=0, tiled=True)  73.8 us
    reduce_scatter x1, waiting for transfers between devices, per_device(): lax.psum_scatter(embedding_part, 'vocab', scatter_dimension=0, tiled=True)  49.5 us
    all_to_all x1, waiting for transfers between devices, per_device(): lax.all_to_all(beam_rows, 'dp', split_axis=1, concat_axis=0, tiled=True)  48.5 us
    all_gather x1, waiting for transfers between devices, per_device(): beam_rows = lax.all_gather(hidden, 'vocab', axis=1, tiled=True)  31.9 us
    ppermute x2, waiting for transfers between devices, per_device(): lax.ppermute(going_up, 'dp', [(d, (d + 1) % ways) for d in range(ways)])  23.2 us
    psum x1, blocking collectives, per_device(): squares = lax.psum(jnp.sum(summed * summed, axis=1), 'dp')  11.7 us
    ppermute x2, starting transfers between devices, per_device(): lax.ppermute(going_up, 'dp', [(d, (d + 1) % ways) for d in range(ways)])  11.5 us
    dot_general x1, matrix products, per_device(): jnp.einsum('bd,vd->bv', beam_columns, out_weight, preferred_element_type=...  9.91 us
  transfers between devices with their start and end apart: 7, of which 6 were waited for; matrix products, arithmetic and copies ran while one was open for 1% of the time, Pallas kernels for 0%

profile of v1, /device:TPU:0, one launch (start us, length us, event | category | flops | bytes accessed | tf_op | source)
XLA Modules:
  0.0 322.5 jit_solution(12057733141031823585)
XLA Ops:
  7.2 0.0 copy-start
  7.2 0.0 all-gather.3.cloned.1.call-start
  7.2 1.8 copy.19
  9.0 0.0 all-gather.3.cloned.1.call-update
  9.0 31.9 %all-gather.3.cloned.1.call-done = bf16[128,8192]{0,1:T(8,128)(2,1)} async-done(((bf16[128,1024]{0,1:T(8,128)(2,1)}), bf16[128,8192]{0,1:T(8,128)(2,1)}) %all-gather.3.cloned.1.call-update) | async-done | bytes 2097168 | tf_op jit(solution)/shard_map/all_gather | solution.py:21
  41.0 4.0 %copy.20 = bf16[128,4,2048]{2,0,1:T(8,128)(2,1)} copy(bf16[128,4,2048]{0,2,1:T(8,128)(2,1)} %bitcast.43) | data formatting | bytes 4194304 | tf_op jit(solution)/shard_map/all_to_all | solution.py:22
  45.0 0.0 copy-start.2
  45.0 4.7 %all-to-all-start = ((bf16[128,4,2048]{2,0,1:T(8,128)(2,1)}), bf16[128,4,2048]{2,0,1:T(8,128)(2,1)S(1)}, u32[]{:S(2)}, u32[]{:S(2)}) async-start(bf16[128,4,2048]{2,0,1:T(8,128)(2,1)} %copy.20), calls=%async_computation | async-start | bytes 4194304 | tf_op jit(solution)/shard_map/all_to_all | solution.py:22
  49.7 0.0 reduce-scatter.3.cloned.1.call-start
  49.7 0.0 copy-done.2
  49.7 0.1 reshape.130
  49.8 48.5 %all-to-all-done = bf16[128,4,2048]{2,0,1:T(8,128)(2,1)S(1)} async-done(((bf16[128,4,2048]{2,0,1:T(8,128)(2,1)}), bf16[128,4,2048]{2,0,1:T(8,128)(2,1)S(1)}, u32[]{:S(2)}, u32[]{:S(2)}) %all-to-all-start) | async-done | bytes 2097184 | tf_op jit(solution)/shard_map/all_to_all | solution.py:22
  98.3 9.9 %fusion.3 = f32[4,128,19,128]{3,1,2,0:T(8,128)} fusion(bf16[19,128,2048,1]{2,1,0,3:T(8,128)(2,1)} %bitcast.51, bf16[128,4,2048]{2,0,1:T(8,128)(2,1)S(1)} %all-to-all-done), kind=kOutput, calls=%fused_computation.5 | convolution fusion | flops 5100273664 | bytes 17039360 | tf_op jit(solution)/shard_map/dense_logits/bd,vd->bv/dot_general | solution.py:24
  108.2 5.3 %gather_fusion = f32[64,128,128]{2,1,0:T(8,128)} fusion(f32[4,128,19,128]{3,1,2,0:T(8,128)} %fusion.3, s32[64]{0:T(128)S(1)} %reshape.130), kind=kCustom, calls=%fused_computation | custom fusion | bytes 8389120 | tf_op jit(solution)/shard_map/dense_logits/gather | solution.py:27
  113.5 0.0 reduce-scatter.3.cloned.1.call-update
  113.5 0.0 reduce-scatter.5.cloned.1.call-start
  113.6 0.0 copy-done
  113.6 0.6 constant_dynamic-slice_fusion
  114.2 0.6 iota_compare_fusion.1
  114.8 73.8 %reduce-scatter.3.cloned.1.call-done = f32[1,16,128,128]{3,2,1,0:T(8,128)} async-done(((f32[4,16,128,128]{3,2,1,0:T(8,128)}), f32[1,16,128,128]{3,2,1,0:T(8,128)}) %reduce-scatter.3.cloned.1.call-update) | async-done | bytes 1048592 | tf_op jit(solution)/shard_map/reduce_scatter | solution.py:28
  188.6 0.0 copy-start.1
  188.6 1.5 select_reduce_fusion
  190.1 1.6 exponential_reduce_fusion
  191.7 8.9 %all-gather = f32[16,1,128]{2,1,0:T(1,128)S(1)} all-gather(f32[2,1,128]{2,1,0:T(1,128)S(1)} %pad_maximum_fusion), channel_id=2, replica_groups=mesh['dp'=4,'vocab'=8] {'vocab'}, dimensions={0}, use_global_device_ids=true | all-gather | bytes 9216 | tf_op jit(solution)/shard_map/softmax_stats/all_gather | solution.py:35
  200.6 0.0 copy-done.1
  200.7 1.4 select_convert_fusion
  202.1 1.5 collective-permute-start
  203.5 2.3 collective-permute-start.1
  205.9 12.8 %collective-permute-done = bf16[1,16,128,128]{3,2,1,0:T(8,128)(2,1)S(1)} collective-permute-done((bf16[1,16,128,128]{3,2,1,0:T(8,128)(2,1)S(1)}, bf16[1,16,128,128]{3,2,1,0:T(8,128)(2,1)S(1)}, u32[]{:S(2)}, u32[]{:S(2)}) %collective-permute-start) | collective-permute-done | bytes 524320 | tf_op jit(solution)/shard_map/ppermute | solution.py:48
  218.7 10.0 %collective-permute-start.2 = (bf16[1,16,128,128]{3,2,1,0:T(8,128)(2,1)S(1)}, bf16[1,16,128,128]{3,2,1,0:T(8,128)(2,1)S(1)}, u32[]{:S(2)}, u32[]{:S(2)}) collective-permute-start(bf16[1,16,128,128]{3,2,1,0:T(8,128)(2,1)S(1)} %collective-permute-done), channel_id=1, source_target_pairs={{0,8},{8,16},{16,24},{24,0},{1,9},{9,17},{17,25},{25,1},{2,10},{10... | collective-permute-start | bytes 1572872 | tf_op jit(solution)/shard_map/ppermute | solution.py:48
  228.7 0.3 broadcast_in_dim.49
  229.0 0.4 copy_dynamic-update-slice_fusion.3
  229.4 0.4 copy_dynamic-update-slice_fusion.2
  229.8 0.0 collective-permute-done.1
  229.8 0.4 copy_dynamic-update-slice_fusion.1
  230.2 10.4 %collective-permute-done.2 = bf16[1,16,128,128]{3,2,1,0:T(8,128)(2,1)S(1)} collective-permute-done((bf16[1,16,128,128]{3,2,1,0:T(8,128)(2,1)S(1)}, bf16[1,16,128,128]{3,2,1,0:T(8,128)(2,1)S(1)}, u32[]{:S(2)}, u32[]{:S(2)}) %collective-permute-start.2) | collective-permute-done | bytes 524320 | tf_op jit(solution)/shard_map/ppermute | solution.py:48
  240.6 0.4 copy_dynamic-update-slice_fusion
  240.9 1.1 convolution_convert_fusion
  242.0 9.5 %fusion = f32[512,2048]{1,0:T(8,128)} fusion(bf16[2432,2048]{1,0:T(8,128)(2,1)} %param.5, bf16[64,8,19,128]{3,2,1,0:T(8,128)(2,1)S(1)} %bitcast.42), kind=kOutput, calls=%fused_computation.1 | convolution fusion | flops 5100273664 | bytes 16646144 | tf_op jit(solution)/shard_map/dense_expected/bv,vd->bd/dot_general | solution.py:65
  251.5 0.0 reduce-scatter.5.cloned.1.call-update
  251.6 49.5 %reduce-scatter.5.cloned.1.call-done = f32[64,2048]{1,0:T(8,128)} async-done(((f32[512,2048]{1,0:T(8,128)}), f32[64,2048]{1,0:T(8,128)}) %reduce-scatter.5.cloned.1.call-update) | async-done | bytes 524304 | tf_op jit(solution)/shard_map/reduce_scatter | solution.py:71
  301.1 1.2 multiply_reduce_fusion
  302.3 11.7 %psum.7 = f32[64]{0:T(128)S(1)} all-reduce(f32[64]{0:T(128)S(1)} %multiply_reduce_fusion), channel_id=1, replica_groups=mesh['dp'=4,'vocab'=8] {'dp'}, use_global_device_ids=true, to_apply=%region_7.8 | all-reduce | flops 64 | bytes 512 | tf_op jit(solution)/shard_map/psum | solution.py:72
  314.0 1.9 broadcast_multiply_fusion
  (7 shorter events, 0.1 us)
Async XLA Ops:
  7.2 106.4 %copy-start = (s32[1,4]{1,0:T(1,128)S(1)}, s32[1,4]{1,0:T(1,128)}, u32[]{:S(2)}) copy-start(s32[1,4]{1,0:T(1,128)} %param.7) | copy-start | bytes 52
  7.2 33.8 %all-gather.3.cloned.1.call-start = ((), (), s32[]{:S(2)}) async-start(), calls=%async_computation.3 | async-start | bytes 2359296 | tf_op jit(solution)/shard_map/all_gather | solution.py:21
  45.0 4.7 %copy-start.2 = (s32[1,4,16]{2,1,0:T(4,128)S(1)}, s32[1,4,16]{2,1,0:T(4,128)}, u32[]{:S(2)}) copy-start(s32[1,4,16]{2,1,0:T(4,128)} %param.6) | copy-start | bytes 772
  45.0 53.3 %all-to-all-start = ((bf16[128,4,2048]{2,0,1:T(8,128)(2,1)}), bf16[128,4,2048]{2,0,1:T(8,128)(2,1)S(1)}, u32[]{:S(2)}, u32[]{:S(2)}) async-start(bf16[128,4,2048]{2,0,1:T(8,128)(2,1)} %copy.20), calls=%async_computation | async-start | bytes 4194304 | tf_op jit(solution)/shard_map/all_to_all | solution.py:22
  49.7 138.9 %reduce-scatter.3.cloned.1.call-start = ((), (), s32[]{:S(2)}) async-start(), calls=%async_computation.4 | async-start | bytes 5242880 | tf_op jit(solution)/shard_map/reduce_scatter | solution.py:28
  113.5 187.6 %reduce-scatter.5.cloned.1.call-start = ((), (), s32[]{:S(2)}) async-start(), calls=%async_computation.5 | async-start | bytes 4718592 | tf_op jit(solution)/shard_map/reduce_scatter | solution.py:71
  188.6 12.1 %copy-start.1 = (f32[1,16,128,128]{3,2,1,0:T(8,128)S(1)}, f32[1,16,128,128]{3,2,1,0:T(8,128)}, u32[]{:S(2)}) copy-start(f32[1,16,128,128]{3,2,1,0:T(8,128)} %reduce-scatter.3.cloned.1.call-done) | copy-start | bytes 3145732
  202.1 16.6 %collective-permute-start = (bf16[1,16,128,128]{3,2,1,0:T(8,128)(2,1)S(1)}, bf16[1,16,128,128]{3,2,1,0:T(8,128)(2,1)S(1)}, u32[]{:S(2)}, u32[]{:S(2)}) collective-permute-start(bf16[1,16,128,128]{3,2,1,0:T(8,128)(2,1)S(1)} %get-tuple-element.2), channel_id=1, source_target_pairs={{0,8},{8,16},{16,24},{24,0},{1,9},{9,17},{17,25},{25,1},{2,10},{10... | collective-permute-start | bytes 1572872 | tf_op jit(solution)/shard_map/ppermute | solution.py:48
  203.5 26.2 %collective-permute-start.1 = (bf16[1,16,128,128]{3,2,1,0:T(8,128)(2,1)S(1)}, bf16[1,16,128,128]{3,2,1,0:T(8,128)(2,1)S(1)}, u32[]{:S(2)}, u32[]{:S(2)}) collective-permute-start(bf16[1,16,128,128]{3,2,1,0:T(8,128)(2,1)S(1)} %get-tuple-element.2), channel_id=1, source_target_pairs={{0,24},{8,0},{16,8},{24,16},{1,25},{9,1},{17,9},{25,17},{2,26},{10... | collective-permute-start | bytes 1572872 | tf_op jit(solution)/shard_map/ppermute | solution.py:53
  218.7 21.8 %collective-permute-start.2 = (bf16[1,16,128,128]{3,2,1,0:T(8,128)(2,1)S(1)}, bf16[1,16,128,128]{3,2,1,0:T(8,128)(2,1)S(1)}, u32[]{:S(2)}, u32[]{:S(2)}) collective-permute-start(bf16[1,16,128,128]{3,2,1,0:T(8,128)(2,1)S(1)} %collective-permute-done), channel_id=1, source_target_pairs={{0,8},{8,16},{16,24},{24,0},{1,9},{9,17},{17,25},{25,1},{2,10},{10... | collective-permute-start | bytes 1572872 | tf_op jit(solution)/shard_map/ppermute | solution.py:48
Sparse Core Ops, SparseCore 0:
  10.4 30.4 all-gather.2
  113.6 74.9 reduce-scatter.2
  251.7 49.3 reduce-scatter.4
